TPU v7x, 32 devices: a whole 2x2x4 slice. The times are simulated.
32 devices in a mesh: seq: 8 (over z, x), exp: 4 (over y, core).
Axes of the slice: x: 2, y: 2, z: 4, core: 2. Of those that a mesh axis runs over, the one named last changes fastest.
Arguments:
- hidden_in: bfloat16 [2048, 1536], P('seq'), may hold values from -6 to 6
- attn_gain: float32 [1536], replicated, may hold values from 0.1 to 1.9
- q_weight: bfloat16 [1536, 1536], P(None, 'exp'), may hold values from -1.25 to 1.25
- k_weight: bfloat16 [1536, 512], P(None, 'exp'), may hold values from -0.625 to 0.625
- v_weight: bfloat16 [1536, 512], P(None, 'exp'), may hold values from -0.15625 to 0.15625
- o_weight: bfloat16 [1536, 1536], P('exp'), may hold values from -0.15625 to 0.15625
- cache_kv: bfloat16 [4096, 1024], P('seq', 'exp'), may hold values from -216 to 216
- moe_gain: float32 [1536], replicated, may hold values from 0.1 to 1.9
- expert_in: bfloat16 [32, 1536, 1024], P('seq'), may hold values from -0.15625 to 0.15625
- expert_out: bfloat16 [32, 512, 1536], P('seq'), may hold values from -0.25 to 0.25
- routes: int32 [2048, 8], P(('seq', 'exp')), may hold values from 0 to 31, all different within a row; in each aligned block of 64 rows (0 to 63, 64 to 127, ...) at most 32 rows name the same one
- route_prob: float32 [2048, 8], P(('seq', 'exp')), may hold values from 0.05 to 1
- page_slot: int32 [256], replicated, may hold values from 0 to 31, as said below
Outputs:
- hidden_out: bfloat16 [2048, 1536], P(('seq', 'exp'))
- decode_pages: bfloat16 [256, 8, 2, 512], P('seq', 'exp')
Inputs may be any that keep to these rules, and one draw needn't show every extreme that they name: `routes`: in each aligned block of 64 rows (the rows of one device) no expert is named by more than 32 rows; a row names 8 different experts. `page_slot`: for each r, the 32 blocks b with b mod (8) == r have different slots.
All inputs are finite; a program needn't handle non-finite values.
Results may differ from a plain program's by a relative error of at most 0.0074.
Values may be sent and summed in bfloat16 or wider, within the bound.
No kernel may reach another device: no remote copies, remote signals or barrier semaphores. Data moves between devices by JAX's collectives and lax.ppermute only.
A program may use at most 128 MiB of HBM per device.

v0:
```python
import math
import jax
import jax.numpy as jnp
from jax import lax
from jax.sharding import PartitionSpec as P

HEADS = 24
KV_HEADS = 8
HEAD_DIM = 64
EXPERTS = 32
PAGE = 8
norm_epsilon = 1e-06
attention_scale = 0.015625
residual_scale = 0.22
masked_score = -1e30


def rms_norm(values, gain_row):
    widened = values.astype(jnp.float32)
    spread = lax.rsqrt(jnp.mean(widened * widened, axis=-1, keepdims=True) + norm_epsilon)
    return (widened * spread * gain_row).astype(jnp.bfloat16)


def attend_block(carried, query_heads, visible, key_rows, value_rows):
    best_old, total_old, summed_old = carried
    scores = (
        jnp.einsum("tkgd,nkd->kgtn", query_heads, key_rows, preferred_element_type=jnp.float32)
        * attention_scale
    )
    scores = jnp.where(visible, scores, masked_score)
    best_new = jnp.maximum(best_old, jnp.max(scores, axis=-1))
    weights = jnp.where(visible, jnp.exp(scores - best_new[..., None]), 0.0)
    factor = jnp.exp(best_old - best_new)
    total_new = total_old * factor + jnp.sum(weights, axis=-1)
    summed_new = summed_old * factor[..., None] + jnp.einsum(
        "kgtn,nkd->kgtd",
        weights.astype(jnp.bfloat16),
        value_rows,
        preferred_element_type=jnp.float32,
    )
    return (best_new, total_new, summed_new)


def block_size(piece_rows):
    return math.gcd(piece_rows, 512)


def body(
    hidden_in,
    attn_gain,
    q_weight,
    k_weight,
    v_weight,
    o_weight,
    cache_kv,
    moe_gain,
    expert_in,
    expert_out,
    routes,
    route_prob,
    page_slot,
):
    seq_count = lax.axis_size("seq")
    seq_index = lax.axis_index("seq")
    exp_index = lax.axis_index("exp")
    tokens_here = hidden_in.shape[0]
    head_dim = HEAD_DIM
    kv_local = k_weight.shape[1] // head_dim
    group_size = HEADS // KV_HEADS
    prompt_len = tokens_here * seq_count // 2
    first_row = seq_index * tokens_here
    query_rows = first_row + jnp.arange(tokens_here, dtype=jnp.int32)
    query_second = query_rows >= prompt_len
    holds_first = first_row < prompt_len
    normed = rms_norm(hidden_in, attn_gain)
    queries = jnp.dot(normed, q_weight, preferred_element_type=jnp.float32).astype(jnp.bfloat16)
    keys_new = jnp.dot(normed, k_weight, preferred_element_type=jnp.float32).astype(jnp.bfloat16)
    values_new = jnp.dot(normed, v_weight, preferred_element_type=jnp.float32).astype(jnp.bfloat16)
    pair_width = 2 * kv_local * head_dim
    pairs_new = jnp.stack(
        [
            keys_new.reshape(tokens_here, kv_local, head_dim),
            values_new.reshape(tokens_here, kv_local, head_dim),
        ],
        axis=2,
    ).reshape(tokens_here, pair_width)
    query_heads = queries.reshape(tokens_here, kv_local, group_size, head_dim)
    cache_lines = cache_kv.reshape(tokens_here, -1)
    blocks_here = tokens_here // PAGE
    rounds = blocks_here // seq_count
    outgoing = pairs_new.reshape(rounds, seq_count, PAGE * pair_width)
    received = lax.all_to_all(outgoing, "seq", split_axis=1, concat_axis=1, tiled=True)
    block_ids = (
        jnp.arange(seq_count, dtype=jnp.int32)[None, :] * blocks_here
        + jnp.arange(rounds, dtype=jnp.int32)[:, None] * seq_count
        + seq_index
    ).reshape(-1)
    table_ids = jnp.arange(page_slot.shape[0], dtype=jnp.int32)
    page_slots = jnp.sum(
        jnp.where(block_ids[:, None] == table_ids[None, :], page_slot[None, :], 0), axis=1
    )
    local_pages = (
        jnp.zeros((blocks_here, PAGE * pair_width), jnp.bfloat16)
        .at[page_slots]
        .set(received.reshape(blocks_here, -1))
    )
    page_rows = local_pages.reshape(blocks_here, PAGE, kv_local, 2, head_dim).transpose(
        0, 2, 3, 1, 4
    )
    page_rows = page_rows.reshape(blocks_here, kv_local, 2, PAGE * head_dim)
    start_state = (
        jnp.full((kv_local, group_size, tokens_here), masked_score, jnp.float32),
        jnp.zeros((kv_local, group_size, tokens_here), jnp.float32),
        jnp.zeros((kv_local, group_size, tokens_here, head_dim), jnp.float32),
    )

    def new_keys_part(carried, new_block, key_first):
        width_rows = new_block.shape[0]
        key_rows = key_first + jnp.arange(width_rows, dtype=jnp.int32)
        visible = ((key_rows >= prompt_len)[None, :] == query_second[:, None]) & (
            key_rows[None, :] <= query_rows[:, None]
        )
        split_pairs = new_block.reshape(width_rows, kv_local, 2, head_dim)
        return lax.cond(
            jnp.any(visible),
            lambda carried_in: attend_block(
                carried_in, query_heads, visible, split_pairs[:, :, 0], split_pairs[:, :, 1]
            ),
            lambda carried_in: carried_in,
            carried,
        )

    carried = start_state
    new_piece = lax.all_gather(pairs_new, "seq", axis=0, tiled=True)
    cache_piece = lax.all_gather(cache_lines, "seq", axis=0, tiled=True)
    piece_rows = new_piece.shape[0]
    stride = block_size(piece_rows)
    new_blocks = new_piece.reshape(piece_rows // stride, stride, -1)
    cache_blocks = cache_piece.reshape(piece_rows // stride, 2 * stride, kv_local, 2, head_dim)
    offsets = stride * jnp.arange(piece_rows // stride, dtype=jnp.int32)
    everything = jnp.ones((tokens_here, 2 * stride), bool)

    def visit(carried_in, block_part):
        new_block, cache_block, key_first = block_part
        carried_in = new_keys_part(carried_in, new_block, key_first)
        carried_in = lax.cond(
            holds_first,
            lambda inner: attend_block(
                inner, query_heads, everything, cache_block[:, :, 0], cache_block[:, :, 1]
            ),
            lambda inner: inner,
            carried_in,
        )
        return (carried_in, None)

    carried, _ = lax.scan(visit, carried, (new_blocks, cache_blocks, offsets))
    best_final, total_final, summed_final = carried
    attended = (
        (summed_final / total_final[..., None])
        .transpose(2, 0, 1, 3)
        .reshape(tokens_here, -1)
        .astype(jnp.bfloat16)
    )
    mixed_rows = lax.psum_scatter(
        jnp.dot(attended, o_weight, preferred_element_type=jnp.float32).astype(jnp.bfloat16),
        "exp",
        scatter_dimension=0,
        tiled=True,
    ).astype(jnp.float32)
    moe_rows = mixed_rows.shape[0]
    residual = (
        lax.dynamic_slice_in_dim(hidden_in, exp_index * moe_rows, moe_rows, 0).astype(jnp.float32)
        + residual_scale * mixed_rows
    )
    moe_in = rms_norm(residual, moe_gain)
    top_count = routes.shape[1]
    assigns = moe_rows * top_count
    capacity = 2 * moe_rows * top_count // EXPERTS
    flat_ids = routes.reshape(-1)
    hit_table = (flat_ids[:, None] == jnp.arange(EXPERTS, dtype=jnp.int32)[None, :]).astype(
        jnp.int32
    )
    earlier = jnp.cumsum(hit_table, axis=0) - hit_table
    slot_rank = jnp.sum(earlier * hit_table, axis=1)
    dest_slot = flat_ids * capacity + slot_rank
    source = (
        jnp.full((EXPERTS * capacity,), assigns, jnp.int32)
        .at[dest_slot]
        .set(jnp.arange(assigns, dtype=jnp.int32))
    )
    filled = source < assigns
    picked = moe_in[jnp.minimum(source, assigns - 1) // top_count]
    dispatched = jnp.where(filled[:, None], picked, jnp.zeros_like(picked)).reshape(
        seq_count, EXPERTS // seq_count, capacity, -1
    )
    hidden = jnp.einsum(
        "sexd,edf->sexf",
        lax.all_to_all(dispatched, "seq", split_axis=0, concat_axis=0, tiled=True),
        expert_in,
        preferred_element_type=jnp.float32,
    )
    half_width = hidden.shape[-1] // 2
    active = (jax.nn.silu(hidden[..., :half_width]) * hidden[..., half_width:]).astype(jnp.bfloat16)
    produced = jnp.einsum(
        "sexf,efd->sexd", active, expert_out, preferred_element_type=jnp.float32
    ).astype(jnp.bfloat16)
    returned = lax.all_to_all(produced, "seq", split_axis=0, concat_axis=0, tiled=True)
    flat_back = returned.reshape(EXPERTS * capacity, -1)
    per_assign = flat_back[dest_slot].reshape(moe_rows, top_count, -1)
    share = route_prob / jnp.sum(route_prob, axis=-1, keepdims=True)
    moe = jnp.sum(share[..., None] * per_assign.astype(jnp.float32), axis=1)
    hidden_out = (residual + residual_scale * moe).astype(jnp.bfloat16)
    return (hidden_out, page_rows)


def solution(mesh):
    return jax.shard_map(
        body,
        mesh=mesh,
        in_specs=(
            P("seq", None),
            P(),
            P(None, "exp"),
            P(None, "exp"),
            P(None, "exp"),
            P("exp", None),
            P("seq", "exp"),
            P(),
            P("seq", None, None),
            P("seq", None, None),
            P(("seq", "exp"), None),
            P(("seq", "exp"), None),
            P(),
        ),
        out_specs=(P(("seq", "exp"), None), P("seq", "exp", None, None)),
        check_vma=False,
    )
```

profile of v0, /device:TPU:0, one launch (start us, length us, event | category | flops | bytes accessed | tf_op | source)
XLA Modules:
  0.0 385.0 jit_solution(13722507623709581729)
XLA Ops:
  7.3 1.5 fusion.45
  8.8 1.7 convolution_convert_fusion.3
  10.5 1.7 convolution_convert_fusion.2
  14.7 40.6 %all-gather.3.cloned.1.call-done = bf16[2048,256]{0,1:T(8,128)(2,1)} async-done(((bf16[256,256]{0,1:T(8,128)(2,1)}), bf16[2048,256]{0,1:T(8,128)(2,1)}) %all-gather.3.cloned.1.call-update) | async-done | bytes 1048592 | tf_op jit(solution)/shard_map/all_gather | solution.py:134
  55.4 1.3 copy.142
  56.7 49.0 %all-gather.5.cloned.1.call-done = bf16[2048,512]{1,0:T(8,128)(2,1)} async-done(((bf16[256,512]{1,0:T(8,128)(2,1)}), bf16[2048,512]{1,0:T(8,128)(2,1)}) %all-gather.5.cloned.1.call-update) | async-done | bytes 2097168 | tf_op jit(solution)/shard_map/all_gather | solution.py:135
  105.7 8.9 %reshape.173 = bf16[4,1024,2,2,64]{4,3,2,1,0:T(2,128)(2,1)} reshape(bf16[2048,512]{1,0:T(8,128)(2,1)} %all-gather.5.cloned.1.call-done) | data formatting | bytes 4194304 | tf_op jit(solution)/shard_map/reshape | solution.py:139
  114.6 10.6 %copy.101 = bf16[4,1024,2,2,64]{1,4,2,3,0:T(8,128)(2,1)} copy(bf16[4,1024,2,2,64]{4,3,2,1,0:T(2,128)(2,1)} %reshape.173) | data formatting | bytes 4194304
  125.3 35.4 %while.16 = (s32[]{:T(128)}, f32[2,3,256]{2,1,0:T(4,128)S(1)}, f32[2,3,256]{2,1,0:T(4,128)S(1)}, f32[2,3,256,64]{2,3,1,0:T(8,128)S(1)}, pred[]{:T(512)}, /*index...) while((s32[]{:T(128)}, f32[2,3,256]{2,1,0:T(4,128)S(1)}, ...), condition=%wide.region_11.12_spmd.clone.clone, body=%wide.region_1.11_spmd.clone.clone.sunk | while | flops 627712256 | bytes 33374036 | solution.py:156
  129.0 2.5 conditional.8
  131.5 4.5 %conditional.9 = ((f32[2,3,256]{2,1,0:T(4,128)S(1)}, f32[2,3,256]{2,1,0:T(4,128)S(1)}, f32[2,3,256,64]{2,3,1,0:T(8,128)S(1)})) conditional(s32[]{:T(128)} %convert_element_type.152, (f32[2,3,256]{2,1,0:T(4,128)S(1)}, f32[2,3,256]{2,1,0:T(4,128)S(1)}, f32[2,3,256,64]{2,3,1,0:T(8,128)S(1)}) %get-tuple-element.445, ...), branch_computations={%region_7.7_spmd, %region_8.10_spmd} | conditional | flops 415435776 | bytes 21532708 | solution.py:146
  139.7 4.5 %conditional.9 = ((f32[2,3,256]{2,1,0:T(4,128)S(1)}, f32[2,3,256]{2,1,0:T(4,128)S(1)}, f32[2,3,256,64]{2,3,1,0:T(8,128)S(1)})) conditional(s32[]{:T(128)} %convert_element_type.152, (f32[2,3,256]{2,1,0:T(4,128)S(1)}, f32[2,3,256]{2,1,0:T(4,128)S(1)}, f32[2,3,256,64]{2,3,1,0:T(8,128)S(1)}) %get-tuple-element.445, ...), branch_computations={%region_7.7_spmd, %region_8.10_spmd} | conditional | flops 415435776 | bytes 21532708 | solution.py:146
  143.0 1.2 fusion.22
  148.0 4.5 %conditional.9 = ((f32[2,3,256]{2,1,0:T(4,128)S(1)}, f32[2,3,256]{2,1,0:T(4,128)S(1)}, f32[2,3,256,64]{2,3,1,0:T(8,128)S(1)})) conditional(s32[]{:T(128)} %convert_element_type.152, (f32[2,3,256]{2,1,0:T(4,128)S(1)}, f32[2,3,256]{2,1,0:T(4,128)S(1)}, f32[2,3,256,64]{2,3,1,0:T(8,128)S(1)}) %get-tuple-element.445, ...), branch_computations={%region_7.7_spmd, %region_8.10_spmd} | conditional | flops 415435776 | bytes 21532708 | solution.py:146
  151.2 1.2 fusion.22
  156.2 4.5 %conditional.9 = ((f32[2,3,256]{2,1,0:T(4,128)S(1)}, f32[2,3,256]{2,1,0:T(4,128)S(1)}, f32[2,3,256,64]{2,3,1,0:T(8,128)S(1)})) conditional(s32[]{:T(128)} %convert_element_type.152, (f32[2,3,256]{2,1,0:T(4,128)S(1)}, f32[2,3,256]{2,1,0:T(4,128)S(1)}, f32[2,3,256,64]{2,3,1,0:T(8,128)S(1)}) %get-tuple-element.445, ...), branch_computations={%region_7.7_spmd, %region_8.10_spmd} | conditional | flops 415435776 | bytes 21532708 | solution.py:146
  160.8 1.5 convolution_convert_fusion
  164.3 2.4 scatter_custom_fusion
  166.9 19.4 %reduce-scatter.2.cloned.1.call-done = bf16[64,1536]{1,0:T(8,128)(2,1)} async-done(((bf16[256,1536]{1,0:T(8,128)(2,1)}), bf16[64,1536]{1,0:T(8,128)(2,1)}) %reduce-scatter.2.cloned.1.call-update) | async-done | bytes 196624 | tf_op jit(solution)/shard_map/reduce_scatter | solution.py:164
  188.5 5.6 %gather_fusion = bf16[1024,1536]{1,0:T(8,128)(2,1)} fusion(bf16[64,1536]{1,0:T(8,128)(2,1)S(1)} %multiply_convert_fusion, s32[1024]{0:T(1024)S(1)} %fusion.59), kind=kCustom, calls=%fused_computation | custom fusion | bytes 6295552 | tf_op jit(solution)/shard_map/gather | solution.py:192
  194.1 3.8 broadcast_select_fusion
  197.9 5.8 %all-to-all-start = ((bf16[8,4,32,1536]{3,2,1,0:T(8,128)(2,1)}), bf16[8,4,32,1536]{3,2,1,0:T(8,128)(2,1)}, u32[]{:S(2)}, u32[]{:S(2)}) async-start(bf16[8,4,32,1536]{3,2,1,0:T(8,128)(2,1)} %broadcast_select_fusion), calls=%async_computation.1 | async-start | bytes 6291456 | tf_op jit(solution)/shard_map/all_to_all | solution.py:198
  204.9 69.6 %all-to-all-done = bf16[8,4,32,1536]{3,2,1,0:T(8,128)(2,1)} async-done(((bf16[8,4,32,1536]{3,2,1,0:T(8,128)(2,1)}), bf16[8,4,32,1536]{3,2,1,0:T(8,128)(2,1)}, u32[]{:S(2)}, u32[]{:S(2)}) %all-to-all-start) | async-done | bytes 3145760 | tf_op jit(solution)/shard_map/all_to_all | solution.py:198
  274.5 3.6 all-to-all-start.2
  278.2 7.4 %fusion.39 = f32[8,4,32,1024]{3,2,0,1:T(8,128)S(1)} fusion(bf16[4,1536,1024]{2,1,0:T(8,128)(2,1)} %param.27, bf16[8,4,32,1536]{3,2,1,0:T(8,128)(2,1)} %all-to-all-done), kind=kOutput, calls=%fused_computation.53 | convolution fusion | flops 3221225472 | bytes 19922944 | tf_op jit(solution)/shard_map/sexd,edf->sexf/dot_general | solution.py:196
  285.6 4.6 %fusion.34 = bf16[8,4,32,1536]{3,2,0,1:T(8,128)(2,1)S(1)} fusion(bf16[4,512,1536]{2,1,0:T(8,128)(2,1)} %param.28, f32[8,4,32,1024]{3,2,0,1:T(8,128)S(1)} %fusion.39), kind=kOutput, calls=%fused_computation.47 | convolution fusion | flops 1615331328 | bytes 13631488 | tf_op jit(solution)/shard_map/sexf,efd->sexd/dot_general | solution.py:204
  290.2 1.9 copy.108
  292.1 6.1 %all-to-all-start.1 = ((bf16[8,4,32,1536]{3,2,1,0:T(8,128)(2,1)}), bf16[8,4,32,1536]{3,2,1,0:T(8,128)(2,1)}, u32[]{:S(2)}, u32[]{:S(2)}) async-start(bf16[8,4,32,1536]{3,2,1,0:T(8,128)(2,1)} %copy.108), calls=%async_computation.2 | async-start | bytes 6291456 | tf_op jit(solution)/shard_map/all_to_all | solution.py:207
  301.4 67.3 %all-to-all-done.1 = bf16[8,4,32,1536]{3,2,1,0:T(8,128)(2,1)} async-done(((bf16[8,4,32,1536]{3,2,1,0:T(8,128)(2,1)}), bf16[8,4,32,1536]{3,2,1,0:T(8,128)(2,1)}, u32[]{:S(2)}, u32[]{:S(2)}) %all-to-all-start.1) | async-done | bytes 3145760 | tf_op jit(solution)/shard_map/all_to_all | solution.py:207
  368.7 5.9 %gather_fusion.1 = bf16[512,1536]{1,0:T(8,128)(2,1)S(1)} fusion(bf16[1024,1536]{1,0:T(8,128)(2,1)} %bitcast.33, s32[1024]{0:T(1024)S(1)} %pad_clamp_fusion), kind=kCustom, calls=%fused_computation.1 | custom fusion | bytes 3147776 | tf_op jit(solution)/shard_map/gather | solution.py:209
  374.6 2.2 fusion.37
  376.8 1.7 add_convert_fusion
  (139 shorter events, 40.8 us)
Async XLA Ops:
  7.2 153.6 %copy-start = (bf16[384,1536]{1,0:T(8,128)(2,1)S(1)}, bf16[384,1536]{1,0:T(8,128)(2,1)}, u32[]{:S(2)}) copy-start(bf16[384,1536]{1,0:T(8,128)(2,1)} %param.24) | copy-start | bytes 3538948
  7.2 6.7 %copy-start.1 = (bf16[256,1536]{1,0:T(8,128)(2,1)S(1)}, bf16[256,1536]{1,0:T(8,128)(2,1)}, u32[]{:S(2)}) copy-start(bf16[256,1536]{1,0:T(8,128)(2,1)} %param.19) | copy-start | bytes 2359300
  7.2 6.7 %copy-start.10 = (f32[1536]{0:T(1024)S(1)}, f32[1536]{0:T(1024)}, u32[]{:S(2)}) copy-start(f32[1536]{0:T(1024)} %param.20) | copy-start | bytes 18436
  7.2 5.8 %copy-start.4 = (bf16[512,256]{1,0:T(8,128)(2,1)S(1)}, bf16[512,256]{1,0:T(8,128)(2,1)}, u32[]{:S(2)}) copy-start(bf16[512,256]{1,0:T(8,128)(2,1)} %param.25) | copy-start | bytes 786436
  7.2 6.7 %copy-start.9 = (bf16[1536,384]{1,0:T(8,128)(2,1)S(1)}, bf16[1536,384]{1,0:T(8,128)(2,1)}, u32[]{:S(2)}) copy-start(bf16[1536,384]{1,0:T(8,128)(2,1)} %param.21) | copy-start | bytes 3538948
  7.2 48.1 %all-gather.3.cloned.1.call-start = ((), (), s32[]{:S(2)}) async-start(), calls=%async_computation.4 | async-start | bytes 1179648 | tf_op jit(solution)/shard_map/all_gather | solution.py:134
  13.0 92.7 %all-gather.5.cloned.1.call-start = ((), (), s32[]{:S(2)}) async-start(), calls=%async_computation.5 | async-start | bytes 2359296 | tf_op jit(solution)/shard_map/all_gather | solution.py:135
  13.9 172.4 %reduce-scatter.2.cloned.1.call-start = ((), (), s32[]{:S(2)}) async-start(), calls=%async_computation.6 | async-start | bytes 983040 | tf_op jit(solution)/shard_map/reduce_scatter | solution.py:164
  160.7 1.6 copy-start.5
  160.7 25.6 %copy-start.2 = (bf16[256,1536]{1,0:T(8,128)(2,1)S(1)}, bf16[256,1536]{1,0:T(8,128)(2,1)}, u32[]{:S(2)}) copy-start(bf16[256,1536]{1,0:T(8,128)(2,1)} %param.19) | copy-start | bytes 2359300
  160.7 26.7 %copy-start.7 = (f32[1536]{0:T(1024)S(1)}, f32[1536]{0:T(1024)}, u32[]{:S(2)}) copy-start(f32[1536]{0:T(1024)} %param.26) | copy-start | bytes 18436
  197.9 5.8 %copy-start.3 = (bf16[256,2,2,64]{0,3,2,1:T(8,128)(2,1)S(1)}, bf16[256,2,2,64]{0,3,2,1:T(8,128)(2,1)}, u32[]{:S(2)}) copy-start(bf16[256,2,2,64]{0,3,2,1:T(8,128)(2,1)} %pad_maximum_fusion) | copy-start | bytes 393220
  197.9 76.6 %all-to-all-start = ((bf16[8,4,32,1536]{3,2,1,0:T(8,128)(2,1)}), bf16[8,4,32,1536]{3,2,1,0:T(8,128)(2,1)}, u32[]{:S(2)}, u32[]{:S(2)}) async-start(bf16[8,4,32,1536]{3,2,1,0:T(8,128)(2,1)} %broadcast_select_fusion), calls=%async_computation.1 | async-start | bytes 6291456 | tf_op jit(solution)/shard_map/all_to_all | solution.py:198
  274.5 17.6 %all-to-all-start.2 = ((bf16[4,8,2048]{2,0,1:T(4,128)(2,1)}), bf16[4,8,2048]{2,0,1:T(4,128)(2,1)S(1)}, u32[]{:S(2)}, u32[]{:S(2)}) async-start(bf16[4,8,2048]{2,0,1:T(4,128)(2,1)} %copy.110), calls=%async_computation.3 | async-start | bytes 262144 | tf_op jit(solution)/shard_map/all_to_all | solution.py:92
  292.1 6.1 %copy-start.6 = (f32[64,8]{0,1:T(8,128)S(1)}, f32[64,8]{0,1:T(8,128)}, u32[]{:S(2)}) copy-start(f32[64,8]{0,1:T(8,128)} %param.30) | copy-start | bytes 6148
  292.1 7.1 %copy-start.8 = (s32[256]{0:T(256)S(1)}, s32[256]{0:T(256)}, u32[]{:S(2)}) copy-start(s32[256]{0:T(256)} %param.31) | copy-start | bytes 3076
  292.1 76.6 %all-to-all-start.1 = ((bf16[8,4,32,1536]{3,2,1,0:T(8,128)(2,1)}), bf16[8,4,32,1536]{3,2,1,0:T(8,128)(2,1)}, u32[]{:S(2)}, u32[]{:S(2)}) async-start(bf16[8,4,32,1536]{3,2,1,0:T(8,128)(2,1)} %copy.108), calls=%async_computation.2 | async-start | bytes 6291456 | tf_op jit(solution)/shard_map/all_to_all | solution.py:207
Sparse Core Ops, SparseCore 0:
  13.1 42.2 all-gather.2
  57.5 48.1 all-gather.4
  162.4 23.8 reduce-scatter.1
where the time goes:
time: 386 us; the launch traced here: 385 us
  waiting for transfers between devices  246 us (64%)
  local copies, waits for them, and re-layouts  49.6 us (13%)
  matrix products  28.3 us (7%)
  other arithmetic  28.1 us (7%)
  starting transfers between devices  15.7 us (4%)
  between operations  14.1 us (4%)
    all_to_all x1, waiting for transfers between devices, body(): lax.all_to_all(dispatched, 'seq', split_axis=0, concat_axis=0, tiled=True)  69.6 us
    all_to_all x1, waiting for transfers between devices, body(): lax.all_to_all(produced, 'seq', split_axis=0, concat_axis=0, tiled=True)  67.3 us
    all_gather x1, waiting for transfers between devices, body(): cache_piece = lax.all_gather(cache_lines, 'seq', axis=0, tiled=True)  49 us
    all_gather x1, waiting for transfers between devices, body(): new_piece = lax.all_gather(pairs_new, 'seq', axis=0, tiled=True)  40.6 us
    reduce_scatter x1, waiting for transfers between devices, body(): lax.psum_scatter(jnp.dot(attended, o_weight, preferred_element_type=jnp.f...  19.4 us
    unnamed x26, local copies, waits for them, and re-layouts  11.7 us
    reshape x1, local copies, waits for them, and re-layouts, body(): cache_piece.reshape(piece_rows // stride, 2 * stride, kv_local, 2, head_dim)  8.88 us
  transfers between devices with their start and end apart: 6, of which 5 were waited for; matrix products, arithmetic and copies ran while one was open for 7% of the time, Pallas kernels for 0%

commit v1 on v0

--- a/solution.py
+++ b/solution.py
@@ -132,7 +132,14 @@
 
     carried = start_state
     new_piece = lax.all_gather(pairs_new, "seq", axis=0, tiled=True)
-    cache_piece = lax.all_gather(cache_lines, "seq", axis=0, tiled=True)
+    size = lax.axis_size("seq")
+    right = [(i, (i + 1) % size) for i in range(size)]
+    pieces = [cache_lines]
+    for far in range(1, size):
+        pieces = [lax.ppermute(pieces[0], "seq", right), *pieces]
+    whole = jnp.concatenate(pieces, axis=0)
+    turn = (lax.axis_index("seq") + 1) * pieces[-1].shape[0]
+    cache_piece = jnp.roll(whole, turn, axis=0)
     piece_rows = new_piece.shape[0]
     stride = block_size(piece_rows)
     new_blocks = new_piece.reshape(piece_rows // stride, stride, -1)

time: 386 us -> 364 us (0.943)
  waiting for transfers between devices: 246 us -> 220 us
    ppermute x0 -> x7, waiting for transfers between devices: none -> 58.2 us  [body(): pieces = [lax.ppermute(pieces[0], 'seq', right), *pieces]]
    all_gather x1 -> x0, waiting for transfers between devices: 49 us -> none  [body(): cache_piece = lax.all_gather(cache_lines, 'seq', axis=0, tiled=True)]
    all_gather x1, waiting for transfers between devices: 40.6 us -> 5.55 us  [body(): new_piece = lax.all_gather(pairs_new, 'seq', axis=0, tiled=True)]
    reshape x1, local copies, waits for them, and re-layouts: 8.88 us -> 3.66 us  [body(): cache_piece.reshape(piece_rows // stride, 2 * stride, kv_local, 2, head_dim)]
    unnamed x26 -> x37, local copies, waits for them, and re-layouts: 11.7 us -> 15.8 us
  transfers between devices with their start and end apart: 6 -> 12, of which waited for: 5 -> 11; matrix products, arithmetic and copies ran while one was open for 7% -> 14% of each run, Pallas kernels for 0% -> 0%
where the time goes in v1:
time: 364 us; the launch traced here: 363 us
  waiting for transfers between devices  220 us (60%)
  local copies, waits for them, and re-layouts  49.7 us (14%)
  matrix products  30.2 us (8%)
  other arithmetic  26.7 us (7%)
  starting transfers between devices  18.5 us (5%)
  between operations  14.5 us (4%)
    all_to_all x1, waiting for transfers between devices, body(): lax.all_to_all(dispatched, 'seq', split_axis=0, concat_axis=0, tiled=True)  69.6 us
    all_to_all x1, waiting for transfers between devices, body(): lax.all_to_all(produced, 'seq', split_axis=0, concat_axis=0, tiled=True)  67.3 us
    ppermute x7, waiting for transfers between devices, body(): pieces = [lax.ppermute(pieces[0], 'seq', right), *pieces]  58.2 us
    reduce_scatter x1, waiting for transfers between devices, body(): lax.psum_scatter(jnp.dot(attended, o_weight, preferred_element_type=jnp.f...  19.8 us
    unnamed x37, local copies, waits for them, and re-layouts  15.8 us
    dot_general x1, matrix products, body(): jnp.einsum('sexd,edf->sexf', lax.all_to_all(dispatched, 'seq', split_axis...  7.37 us
  transfers between devices with their start and end apart: 12, of which 11 were waited for; matrix products, arithmetic and copies ran while one was open for 14% of the time, Pallas kernels for 0%

profile of v1, /device:TPU:0, one launch (start us, length us, event | category | flops | bytes accessed | tf_op | source)
XLA Modules:
  0.0 363.0 jit_solution(15823525190630028653)
XLA Ops:
  8.4 3.0 collective-permute-start
  11.4 9.3 %collective-permute-done = bf16[256,512]{1,0:T(8,128)(2,1)S(1)} collective-permute-done((bf16[256,512]{1,0:T(8,128)(2,1)S(1)}, bf16[256,512]{1,0:T(8,128)(2,1)S(1)}, u32[]{:S(2)}, u32[]{:S(2)}) %collective-permute-start) | collective-permute-done | bytes 262176 | tf_op jit(solution)/shard_map/ppermute | solution.py:139
  20.8 10.2 %collective-permute-done.1 = bf16[256,512]{1,0:T(8,128)(2,1)S(1)} collective-permute-done((bf16[256,512]{1,0:T(8,128)(2,1)S(1)}, bf16[256,512]{1,0:T(8,128)(2,1)S(1)}, u32[]{:S(2)}, u32[]{:S(2)}) %collective-permute-start.1) | collective-permute-done | bytes 262176 | tf_op jit(solution)/shard_map/ppermute | solution.py:139
  30.9 9.3 %collective-permute-done.2 = bf16[256,512]{1,0:T(8,128)(2,1)S(1)} collective-permute-done((bf16[256,512]{1,0:T(8,128)(2,1)S(1)}, bf16[256,512]{1,0:T(8,128)(2,1)S(1)}, u32[]{:S(2)}, u32[]{:S(2)}) %collective-permute-start.2) | collective-permute-done | bytes 262176 | tf_op jit(solution)/shard_map/ppermute | solution.py:139
  41.6 7.7 %collective-permute-done.3 = bf16[256,512]{1,0:T(8,128)(2,1)S(1)} collective-permute-done((bf16[256,512]{1,0:T(8,128)(2,1)S(1)}, bf16[256,512]{1,0:T(8,128)(2,1)S(1)}, u32[]{:S(2)}, u32[]{:S(2)}) %collective-permute-start.3) | collective-permute-done | bytes 262176 | tf_op jit(solution)/shard_map/ppermute | solution.py:139
  51.0 7.3 %collective-permute-done.4 = bf16[256,512]{1,0:T(8,128)(2,1)S(1)} collective-permute-done((bf16[256,512]{1,0:T(8,128)(2,1)S(1)}, bf16[256,512]{1,0:T(8,128)(2,1)S(1)}, u32[]{:S(2)}, u32[]{:S(2)}) %collective-permute-start.4) | collective-permute-done | bytes 262176 | tf_op jit(solution)/shard_map/ppermute | solution.py:139
  60.8 7.0 %collective-permute-done.5 = bf16[256,512]{1,0:T(8,128)(2,1)} collective-permute-done((bf16[256,512]{1,0:T(8,128)(2,1)S(1)}, bf16[256,512]{1,0:T(8,128)(2,1)}, u32[]{:S(2)}, u32[]{:S(2)}) %collective-permute-start.5) | collective-permute-done | bytes 262176 | tf_op jit(solution)/shard_map/ppermute | solution.py:139
  67.9 2.6 convolution_convert_fusion.1
  71.6 7.4 %collective-permute-done.6 = bf16[256,512]{1,0:T(8,128)(2,1)} collective-permute-done((bf16[256,512]{1,0:T(8,128)(2,1)}, bf16[256,512]{1,0:T(8,128)(2,1)}, u32[]{:S(2)}, u32[]{:S(2)}) %collective-permute-start.6) | collective-permute-done | bytes 262176 | tf_op jit(solution)/shard_map/ppermute | solution.py:139
  83.3 3.7 %reshape.173 = bf16[4,1024,2,2,64]{4,3,2,1,0:T(2,128)(2,1)} reshape(bf16[2048,512]{1,0:T(8,128)(2,1)S(1)} %constant_dynamic-slice_fusion.1) | data formatting | bytes 4194304 | tf_op jit(solution)/shard_map/reshape | solution.py:146
  87.0 10.7 %copy.101 = bf16[4,1024,2,2,64]{1,4,2,3,0:T(8,128)(2,1)} copy(bf16[4,1024,2,2,64]{4,3,2,1,0:T(2,128)(2,1)} %reshape.173) | data formatting | bytes 4194304
  97.6 5.5 %all-gather.2.cloned.1.call-done = bf16[2048,256]{0,1:T(8,128)(2,1)} async-done(((bf16[256,256]{0,1:T(8,128)(2,1)}), bf16[2048,256]{0,1:T(8,128)(2,1)}) %all-gather.2.cloned.1.call-update) | async-done | bytes 1048592 | tf_op jit(solution)/shard_map/all_gather | solution.py:134
  104.6 33.4 %while.16 = (s32[]{:T(128)}, f32[2,3,256]{2,1,0:T(4,128)S(1)}, f32[2,3,256]{2,1,0:T(4,128)S(1)}, f32[2,3,256,64]{2,3,1,0:T(8,128)S(1)}, pred[]{:T(512)}, /*index...) while((s32[]{:T(128)}, f32[2,3,256]{2,1,0:T(4,128)S(1)}, ...), condition=%wide.region_11.12_spmd.clone.clone, body=%wide.region_1.11_spmd.clone.clone.sunk | while | flops 627712256 | bytes 33374036 | solution.py:163
  107.8 2.5 conditional.8
  110.3 4.5 %conditional.9 = ((f32[2,3,256]{2,1,0:T(4,128)S(1)}, f32[2,3,256]{2,1,0:T(4,128)S(1)}, f32[2,3,256,64]{2,3,1,0:T(8,128)S(1)})) conditional(s32[]{:T(128)} %convert_element_type.152, (f32[2,3,256]{2,1,0:T(4,128)S(1)}, f32[2,3,256]{2,1,0:T(4,128)S(1)}, f32[2,3,256,64]{2,3,1,0:T(8,128)S(1)}) %get-tuple-element.445, ...), branch_computations={%region_7.7_spmd, %region_8.10_spmd} | conditional | flops 415435776 | bytes 21532708 | solution.py:153
  118.0 4.5 %conditional.9 = ((f32[2,3,256]{2,1,0:T(4,128)S(1)}, f32[2,3,256]{2,1,0:T(4,128)S(1)}, f32[2,3,256,64]{2,3,1,0:T(8,128)S(1)})) conditional(s32[]{:T(128)} %convert_element_type.152, (f32[2,3,256]{2,1,0:T(4,128)S(1)}, f32[2,3,256]{2,1,0:T(4,128)S(1)}, f32[2,3,256,64]{2,3,1,0:T(8,128)S(1)}) %get-tuple-element.445, ...), branch_computations={%region_7.7_spmd, %region_8.10_spmd} | conditional | flops 415435776 | bytes 21532708 | solution.py:153
  125.8 4.5 %conditional.9 = ((f32[2,3,256]{2,1,0:T(4,128)S(1)}, f32[2,3,256]{2,1,0:T(4,128)S(1)}, f32[2,3,256,64]{2,3,1,0:T(8,128)S(1)})) conditional(s32[]{:T(128)} %convert_element_type.152, (f32[2,3,256]{2,1,0:T(4,128)S(1)}, f32[2,3,256]{2,1,0:T(4,128)S(1)}, f32[2,3,256,64]{2,3,1,0:T(8,128)S(1)}) %get-tuple-element.445, ...), branch_computations={%region_7.7_spmd, %region_8.10_spmd} | conditional | flops 415435776 | bytes 21532708 | solution.py:153
  133.5 4.5 %conditional.9 = ((f32[2,3,256]{2,1,0:T(4,128)S(1)}, f32[2,3,256]{2,1,0:T(4,128)S(1)}, f32[2,3,256,64]{2,3,1,0:T(8,128)S(1)})) conditional(s32[]{:T(128)} %convert_element_type.152, (f32[2,3,256]{2,1,0:T(4,128)S(1)}, f32[2,3,256]{2,1,0:T(4,128)S(1)}, f32[2,3,256,64]{2,3,1,0:T(8,128)S(1)}) %get-tuple-element.445, ...), branch_computations={%region_7.7_spmd, %region_8.10_spmd} | conditional | flops 415435776 | bytes 21532708 | solution.py:153
  141.6 2.6 scatter_custom_fusion
  144.4 19.8 %reduce-scatter.2.cloned.1.call-done = bf16[64,1536]{1,0:T(8,128)(2,1)} async-done(((bf16[256,1536]{1,0:T(8,128)(2,1)}), bf16[64,1536]{1,0:T(8,128)(2,1)}) %reduce-scatter.2.cloned.1.call-update) | async-done | bytes 196624 | tf_op jit(solution)/shard_map/reduce_scatter | solution.py:171
  166.3 5.6 %gather_fusion = bf16[1024,1536]{1,0:T(8,128)(2,1)} fusion(bf16[64,1536]{1,0:T(8,128)(2,1)S(1)} %multiply_convert_fusion, s32[1024]{0:T(1024)S(1)} %fusion.59), kind=kCustom, calls=%fused_computation | custom fusion | bytes 6295552 | tf_op jit(solution)/shard_map/gather | solution.py:199
  171.9 3.8 %broadcast_select_fusion = bf16[8,4,32,1536]{3,2,1,0:T(8,128)(2,1)} fusion(bf16[8,4,32,1536]{3,2,1,0:T(8,128)(2,1)} %bitcast.141, pred[8,4,32]{2,1,0:T(4,128)(4,1)S(1)} %broadcast_in_dim.86), kind=kLoop, calls=%fused_computation.51 | loop fusion | flops 1572864 | bytes 6292480 | tf_op jit(solution)/shard_map/jit(_where)/select_n | solution.py:200
  175.7 5.7 %all-to-all-start = ((bf16[8,4,32,1536]{3,2,1,0:T(8,128)(2,1)}), bf16[8,4,32,1536]{3,2,1,0:T(8,128)(2,1)}, u32[]{:S(2)}, u32[]{:S(2)}) async-start(bf16[8,4,32,1536]{3,2,1,0:T(8,128)(2,1)} %broadcast_select_fusion), calls=%async_computation.1 | async-start | bytes 6291456 | tf_op jit(solution)/shard_map/all_to_all | solution.py:205
  182.6 69.6 %all-to-all-done = bf16[8,4,32,1536]{3,2,1,0:T(8,128)(2,1)} async-done(((bf16[8,4,32,1536]{3,2,1,0:T(8,128)(2,1)}), bf16[8,4,32,1536]{3,2,1,0:T(8,128)(2,1)}, u32[]{:S(2)}, u32[]{:S(2)}) %all-to-all-start) | async-done | bytes 3145760 | tf_op jit(solution)/shard_map/all_to_all | solution.py:205
  252.2 3.6 %all-to-all-start.2 = ((bf16[4,8,2048]{2,0,1:T(4,128)(2,1)}), bf16[4,8,2048]{2,0,1:T(4,128)(2,1)S(1)}, u32[]{:S(2)}, u32[]{:S(2)}) async-start(bf16[4,8,2048]{2,0,1:T(4,128)(2,1)} %copy.110), calls=%async_computation.3 | async-start | bytes 262144 | tf_op jit(solution)/shard_map/all_to_all | solution.py:92
  255.8 7.4 %fusion.39 = f32[8,4,32,1024]{3,2,0,1:T(8,128)S(1)} fusion(bf16[4,1536,1024]{2,1,0:T(8,128)(2,1)} %param.27, bf16[8,4,32,1536]{3,2,1,0:T(8,128)(2,1)} %all-to-all-done), kind=kOutput, calls=%fused_computation.53 | convolution fusion | flops 3221225472 | bytes 19922944 | tf_op jit(solution)/shard_map/sexd,edf->sexf/dot_general | solution.py:203
  263.2 4.6 %fusion.34 = bf16[8,4,32,1536]{3,2,0,1:T(8,128)(2,1)S(1)} fusion(bf16[4,512,1536]{2,1,0:T(8,128)(2,1)} %param.28, f32[8,4,32,1024]{3,2,0,1:T(8,128)S(1)} %fusion.39), kind=kOutput, calls=%fused_computation.47 | convolution fusion | flops 1615331328 | bytes 13631488 | tf_op jit(solution)/shard_map/sexf,efd->sexd/dot_general | solution.py:211
  267.8 1.9 copy.108
  269.8 6.1 %all-to-all-start.1 = ((bf16[8,4,32,1536]{3,2,1,0:T(8,128)(2,1)}), bf16[8,4,32,1536]{3,2,1,0:T(8,128)(2,1)}, u32[]{:S(2)}, u32[]{:S(2)}) async-start(bf16[8,4,32,1536]{3,2,1,0:T(8,128)(2,1)} %copy.108), calls=%async_computation.2 | async-start | bytes 6291456 | tf_op jit(solution)/shard_map/all_to_all | solution.py:214
  279.0 67.3 %all-to-all-done.1 = bf16[8,4,32,1536]{3,2,1,0:T(8,128)(2,1)} async-done(((bf16[8,4,32,1536]{3,2,1,0:T(8,128)(2,1)}), bf16[8,4,32,1536]{3,2,1,0:T(8,128)(2,1)}, u32[]{:S(2)}, u32[]{:S(2)}) %all-to-all-start.1) | async-done | bytes 3145760 | tf_op jit(solution)/shard_map/all_to_all | solution.py:214
  346.3 5.9 %gather_fusion.1 = bf16[512,1536]{1,0:T(8,128)(2,1)S(1)} fusion(bf16[1024,1536]{1,0:T(8,128)(2,1)} %bitcast.33, s32[1024]{0:T(1024)S(1)} %pad_clamp_fusion), kind=kCustom, calls=%fused_computation.1 | custom fusion | bytes 3147776 | tf_op jit(solution)/shard_map/gather | solution.py:216
  352.2 2.2 fusion.37
  (163 shorter events, 55.9 us)
Async XLA Ops:
  7.2 130.9 %copy-start = (bf16[384,1536]{1,0:T(8,128)(2,1)S(1)}, bf16[384,1536]{1,0:T(8,128)(2,1)}, u32[]{:S(2)}) copy-start(bf16[384,1536]{1,0:T(8,128)(2,1)} %param.24) | copy-start | bytes 3538948
  7.2 60.7 %copy-start.1 = (bf16[256,1536]{1,0:T(8,128)(2,1)S(1)}, bf16[256,1536]{1,0:T(8,128)(2,1)}, u32[]{:S(2)}) copy-start(bf16[256,1536]{1,0:T(8,128)(2,1)} %param.19) | copy-start | bytes 2359300
  7.2 60.7 %copy-start.8 = (f32[1536]{0:T(1024)S(1)}, f32[1536]{0:T(1024)}, u32[]{:S(2)}) copy-start(f32[1536]{0:T(1024)} %param.20) | copy-start | bytes 18436
  7.2 96.0 %all-gather.2.cloned.1.call-start = ((), (), s32[]{:S(2)}) async-start(), calls=%async_computation.4 | async-start | bytes 1179648 | tf_op jit(solution)/shard_map/all_gather | solution.py:134
  8.4 12.3 %collective-permute-start = (bf16[256,512]{1,0:T(8,128)(2,1)S(1)}, bf16[256,512]{1,0:T(8,128)(2,1)S(1)}, u32[]{:S(2)}, u32[]{:S(2)}) collective-permute-start(bf16[256,512]{1,0:T(8,128)(2,1)S(1)} %reshape.172), channel_id=1, source_target_pairs={{0,4},{4,8},{8,12},{12,16},{16,20},{20,24},{24,28},{28,0},{1,5},{5... | collective-permute-start | bytes 786440 | tf_op jit(solution)/shard_map/ppermute | solution.py:139
  20.8 10.2 %collective-permute-start.1 = (bf16[256,512]{1,0:T(8,128)(2,1)S(1)}, bf16[256,512]{1,0:T(8,128)(2,1)S(1)}, u32[]{:S(2)}, u32[]{:S(2)}) collective-permute-start(bf16[256,512]{1,0:T(8,128)(2,1)S(1)} %collective-permute-done), channel_id=1, source_target_pairs={{0,4},{4,8},{8,12},{12,16},{16,20},{20,24},{24,28},{28,0},{1,5},{5... | collective-permute-start | bytes 786440 | tf_op jit(solution)/shard_map/ppermute | solution.py:139
  30.9 9.3 %collective-permute-start.2 = (bf16[256,512]{1,0:T(8,128)(2,1)S(1)}, bf16[256,512]{1,0:T(8,128)(2,1)S(1)}, u32[]{:S(2)}, u32[]{:S(2)}) collective-permute-start(bf16[256,512]{1,0:T(8,128)(2,1)S(1)} %collective-permute-done.1), channel_id=1, source_target_pairs={{0,4},{4,8},{8,12},{12,16},{16,20},{20,24},{24,28},{28,0},{1,5},{5... | collective-permute-start | bytes 786440 | tf_op jit(solution)/shard_map/ppermute | solution.py:139
  40.2 9.1 %collective-permute-start.3 = (bf16[256,512]{1,0:T(8,128)(2,1)S(1)}, bf16[256,512]{1,0:T(8,128)(2,1)S(1)}, u32[]{:S(2)}, u32[]{:S(2)}) collective-permute-start(bf16[256,512]{1,0:T(8,128)(2,1)S(1)} %collective-permute-done.2), channel_id=1, source_target_pairs={{0,4},{4,8},{8,12},{12,16},{16,20},{20,24},{24,28},{28,0},{1,5},{5... | collective-permute-start | bytes 786440 | tf_op jit(solution)/shard_map/ppermute | solution.py:139
  49.3 9.1 %collective-permute-start.4 = (bf16[256,512]{1,0:T(8,128)(2,1)S(1)}, bf16[256,512]{1,0:T(8,128)(2,1)S(1)}, u32[]{:S(2)}, u32[]{:S(2)}) collective-permute-start(bf16[256,512]{1,0:T(8,128)(2,1)S(1)} %collective-permute-done.3), channel_id=1, source_target_pairs={{0,4},{4,8},{8,12},{12,16},{16,20},{20,24},{24,28},{28,0},{1,5},{5... | collective-permute-start | bytes 786440 | tf_op jit(solution)/shard_map/ppermute | solution.py:139
  58.4 9.5 %collective-permute-start.5 = (bf16[256,512]{1,0:T(8,128)(2,1)S(1)}, bf16[256,512]{1,0:T(8,128)(2,1)}, u32[]{:S(2)}, u32[]{:S(2)}) collective-permute-start(bf16[256,512]{1,0:T(8,128)(2,1)S(1)} %collective-permute-done.4), channel_id=1, source_target_pairs={{0,4},{4,8},{8,12},{12,16},{16,20},{20,24},{24,28},{28,0},{1,5},{5... | collective-permute-start | bytes 786440 | tf_op jit(solution)/shard_map/ppermute | solution.py:139
  60.8 103.3 %reduce-scatter.2.cloned.1.call-start = ((), (), s32[]{:S(2)}) async-start(), calls=%async_computation.5 | async-start | bytes 983040 | tf_op jit(solution)/shard_map/reduce_scatter | solution.py:171
  67.9 11.1 %collective-permute-start.6 = (bf16[256,512]{1,0:T(8,128)(2,1)}, bf16[256,512]{1,0:T(8,128)(2,1)}, u32[]{:S(2)}, u32[]{:S(2)}) collective-permute-start(bf16[256,512]{1,0:T(8,128)(2,1)} %collective-permute-done.5), channel_id=1, source_target_pairs={{0,4},{4,8},{8,12},{12,16},{16,20},{20,24},{24,28},{28,0},{1,5},{5... | collective-permute-start | bytes 786440 | tf_op jit(solution)/shard_map/ppermute | solution.py:139
  138.0 1.6 copy-start.4
  138.0 26.1 %copy-start.2 = (bf16[256,1536]{1,0:T(8,128)(2,1)S(1)}, bf16[256,1536]{1,0:T(8,128)(2,1)}, u32[]{:S(2)}) copy-start(bf16[256,1536]{1,0:T(8,128)(2,1)} %param.19) | copy-start | bytes 2359300
  138.0 27.2 %copy-start.6 = (f32[1536]{0:T(1024)S(1)}, f32[1536]{0:T(1024)}, u32[]{:S(2)}) copy-start(f32[1536]{0:T(1024)} %param.26) | copy-start | bytes 18436
  175.7 5.7 %copy-start.3 = (bf16[256,2,2,64]{0,3,2,1:T(8,128)(2,1)S(1)}, bf16[256,2,2,64]{0,3,2,1:T(8,128)(2,1)}, u32[]{:S(2)}) copy-start(bf16[256,2,2,64]{0,3,2,1:T(8,128)(2,1)} %pad_maximum_fusion) | copy-start | bytes 393220
  175.7 76.5 %all-to-all-start = ((bf16[8,4,32,1536]{3,2,1,0:T(8,128)(2,1)}), bf16[8,4,32,1536]{3,2,1,0:T(8,128)(2,1)}, u32[]{:S(2)}, u32[]{:S(2)}) async-start(bf16[8,4,32,1536]{3,2,1,0:T(8,128)(2,1)} %broadcast_select_fusion), calls=%async_computation.1 | async-start | bytes 6291456 | tf_op jit(solution)/shard_map/all_to_all | solution.py:205
  252.2 17.6 %all-to-all-start.2 = ((bf16[4,8,2048]{2,0,1:T(4,128)(2,1)}), bf16[4,8,2048]{2,0,1:T(4,128)(2,1)S(1)}, u32[]{:S(2)}, u32[]{:S(2)}) async-start(bf16[4,8,2048]{2,0,1:T(4,128)(2,1)} %copy.110), calls=%async_computation.3 | async-start | bytes 262144 | tf_op jit(solution)/shard_map/all_to_all | solution.py:92
  269.8 6.1 %copy-start.5 = (f32[64,8]{0,1:T(8,128)S(1)}, f32[64,8]{0,1:T(8,128)}, u32[]{:S(2)}) copy-start(f32[64,8]{0,1:T(8,128)} %param.30) | copy-start | bytes 6148
  269.8 7.1 %copy-start.7 = (s32[256]{0:T(256)S(1)}, s32[256]{0:T(256)}, u32[]{:S(2)}) copy-start(s32[256]{0:T(256)} %param.31) | copy-start | bytes 3076
  269.8 76.6 %all-to-all-start.1 = ((bf16[8,4,32,1536]{3,2,1,0:T(8,128)(2,1)}), bf16[8,4,32,1536]{3,2,1,0:T(8,128)(2,1)}, u32[]{:S(2)}, u32[]{:S(2)}) async-start(bf16[8,4,32,1536]{3,2,1,0:T(8,128)(2,1)} %copy.108), calls=%async_computation.2 | async-start | bytes 6291456 | tf_op jit(solution)/shard_map/all_to_all | solution.py:214
Sparse Core Ops, SparseCore 0:
  60.9 42.2 all-gather.1
  139.7 24.3 reduce-scatter.1
